TPU v7x, 32 devices: a whole 2x2x4 slice. The times are simulated.
32 devices in a mesh: ctx: 4 (over z), row: 8 (over y, x, core).
Axes of the slice: x: 2, y: 2, z: 4, core: 2. Of those that a mesh axis runs over, the one named last changes fastest.
Arguments:
- queries: bfloat16 [2048, 2048], P('row'), may hold values from -120 to 120
- keys: bfloat16 [1536, 2048], P('ctx'), may hold values from -5 to 5
- values: bfloat16 [1536, 2048], P('ctx'), may hold values from -6 to 6
- block_list: int32 [16, 8], P('row'), may hold values from 0 to 11, as said below
- block_count: int32 [16], P('row'), may hold values from 1 to 8, as said below
Outputs:
- owned: bfloat16 [2048, 2048], P('row', 'ctx')
Inputs may be any that keep to these rules, and one draw needn't show every extreme that they name: `block_list`: entries of one list are distinct; the first entry of the list of query block b is b % 12. Entries past block_count are ignored. `block_count`: every query block uses at least one list entry.
All inputs are finite; a program needn't handle non-finite values.
Results may differ from a plain program's by a relative error of at most 0.0044.
Values may be sent and summed in bfloat16 or wider, within the bound.
No kernel may reach another device: no remote copies, remote signals or barrier semaphores. Data moves between devices by JAX's collectives and lax.ppermute only.
A program may use at most 64 MiB of HBM per device.

v0:
```python
import jax
import jax.numpy as jnp
from jax import lax
from jax.sharding import PartitionSpec as P

HEADS = 16
HEAD_DIM = 128
BLOCK = 128
masked_fill = -1e30


def combine_rows(pieces):
    maxima, totals, partial_out = pieces
    item_rows, sources, head_share = maxima.shape
    row_best = jnp.max(maxima, axis=1)
    weight = jnp.exp(maxima - row_best[:, None, :])
    total_sum = jnp.sum(totals * weight, axis=1)
    out_heads = partial_out.reshape(item_rows, sources, head_share, HEAD_DIM)
    numerator = jnp.sum(out_heads * weight[:, :, :, None], axis=1)
    return (numerator / total_sum[:, :, None]).reshape(item_rows, head_share * HEAD_DIM)


def chosen_range(block_list, block_count, first_block, block_span):
    slot_live = jnp.arange(block_list.shape[1], dtype=jnp.int32)[None, :] < block_count[:, None]
    block_ids = first_block + jnp.arange(block_span, dtype=jnp.int32)
    block_hits = (block_list[:, :, None] == block_ids[None, None, :]) & slot_live[:, :, None]
    return jnp.any(block_hits, axis=1)


def segment_parts(query_heads, key_heads, value_heads, chosen):
    key_live = jnp.repeat(jnp.repeat(chosen, BLOCK, axis=0), BLOCK, axis=1)[None, :, :]
    score_scale = 1.0 / HEAD_DIM**0.5
    scores = (
        jnp.einsum("qhd,khd->hqk", query_heads, key_heads, preferred_element_type=jnp.float32)
        * score_scale
    )
    seg_max = jnp.max(jnp.where(key_live, scores, masked_fill), axis=2)
    probs_live = jnp.where(key_live, jnp.exp(scores - seg_max[:, :, None]), 0.0)
    seg_total = jnp.sum(probs_live, axis=2)
    probs_low = probs_live.astype(jnp.bfloat16)
    seg_out = jnp.einsum("hqk,khd->qhd", probs_low, value_heads, preferred_element_type=jnp.float32)
    return (seg_max, seg_total, seg_out)


def local_parts(queries, keys, values, block_list, block_count):
    row_count = queries.shape[0]
    ctx_span = keys.shape[0]
    blocks_here = ctx_span // BLOCK
    chosen = chosen_range(block_list, block_count, lax.axis_index("ctx") * blocks_here, blocks_here)
    return segment_parts(
        queries.reshape(row_count, HEADS, HEAD_DIM),
        keys.reshape(ctx_span, HEADS, HEAD_DIM),
        values.reshape(ctx_span, HEADS, HEAD_DIM),
        chosen,
    )


def local(queries, keys, values, block_list, block_count):
    row_count = queries.shape[0]
    shards = lax.axis_size("ctx")
    head_share = HEADS // shards
    share_width = head_share * HEAD_DIM
    seg_max, seg_total, seg_out = local_parts(queries, keys, values, block_list, block_count)
    sent = (
        jnp.transpose(seg_max)[:, None, :],
        jnp.transpose(seg_total)[:, None, :],
        seg_out.reshape(row_count, 1, HEADS * HEAD_DIM),
    )
    attended = combine_rows(
        (
            lax.all_to_all(sent[0], "ctx", split_axis=2, concat_axis=1, tiled=True),
            lax.all_to_all(sent[1], "ctx", split_axis=2, concat_axis=1, tiled=True),
            lax.all_to_all(sent[2], "ctx", split_axis=2, concat_axis=1, tiled=True),
        )
    )
    attended_low = attended.astype(jnp.bfloat16)
    owners = lax.axis_size("row")
    per_owner = row_count // owners
    grouped = attended_low.reshape(per_owner, owners, share_width)
    regrouped = lax.all_to_all(grouped, "row", split_axis=1, concat_axis=0, tiled=True)
    return regrouped.reshape(row_count, share_width)


def solution(mesh):
    return jax.shard_map(
        local,
        mesh=mesh,
        in_specs=(P("row", None), P("ctx", None), P("ctx", None), P("row", None), P("row")),
        out_specs=P("row", "ctx"),
        check_vma=False,
    )
```

profile of v0, /device:TPU:0, one launch (start us, length us, event | category | flops | bytes accessed | tf_op | source)
XLA Modules:
  0.0 105.7 jit_solution(18359404160349722766)
XLA Ops:
  0.0 0.8 iota_compare_fusion
  0.9 0.9 and_reduce_fusion
  1.8 0.2 copy.27
  2.0 5.2 %select_reduce_fusion = (f32[16,256]{1,0:T(8,128)S(1)}, f32[16,256,384]{2,1,0:T(8,128)}) fusion(pred[256,384]{1,0:T(8,128)(4,1)S(1)} %copy.27, bf16[384,2048]{1,0:T(8,128)(2,1)S(1)} %copy-done, bf16[256,2048]{1,0:T(8,128)(2,1)} %param.5), kind=kOutput, calls=%fused_computation.1 | convolution fusion | flops 407367680 | bytes 9027584 | tf_op jit(solution)/shard_map/qhd,khd->hqk/dot_general | solution.py:34
  7.2 0.6 broadcast_in_dim.47
  7.9 6.3 %all-to-all-start.1 = ((f32[256,1,16]{0,1,2:T(1,128)}), f32[256,1,16]{0,1,2:T(1,128)S(1)}, u32[]{:S(2)}, u32[]{:S(2)}) async-start(f32[256,1,16]{0,1,2:T(1,128)} %broadcast_in_dim.47), calls=%async_computation.1 | async-start | bytes 32768 | tf_op jit(solution)/shard_map/all_to_all | solution.py:71
  14.2 4.0 %fusion = f32[16,256]{1,0:T(8,128)S(1)} fusion(f32[16,256,384]{2,1,0:T(8,128)} %get-tuple-element.8, f32[16,256]{1,0:T(8,128)S(1)} %get-tuple-element.7, pred[256,384]{1,0:T(8,128)(4,1)S(1)} %copy.27), kind=kLoop, calls=%fused_computation.2 | loop fusion | flops 6287360 | bytes 6422528 | tf_op jit(solution)/shard_map/reduce_sum | solution.py:39
  18.2 1.6 %copy.36 = bf16[384,2048]{0,1:T(8,128)(2,1)} copy(bf16[384,2048]{1,0:T(8,128)(2,1)S(1)} %copy-done.1) | data formatting | bytes 3145728 | tf_op jit(solution)/shard_map/reshape | solution.py:53
  19.7 0.6 broadcast_in_dim.48
  20.3 5.1 %all-to-all-start.2 = ((f32[256,1,16]{0,1,2:T(1,128)}), f32[256,1,16]{0,1,2:T(1,128)S(1)}, u32[]{:S(2)}, u32[]{:S(2)}) async-start(f32[256,1,16]{0,1,2:T(1,128)} %broadcast_in_dim.48), calls=%async_computation.2 | async-start | bytes 32768 | tf_op jit(solution)/shard_map/all_to_all | solution.py:72
  25.4 4.2 %fusion.2 = f32[16,256,128]{1,2,0:T(8,128)S(1)} fusion(bf16[384,16,128]{0,2,1:T(8,128)(2,1)} %bitcast.49, f32[16,256,384]{2,1,0:T(8,128)} %get-tuple-element.8, f32[16,256]{1,0:T(8,128)S(1)} %get-tuple-element.7, pred[256,384]{1,0:T(8,128)(4,1)S(1)} %copy.27), kind=kOutput, calls=%fused_computation.4 | convolution fusion | flops 408944640 | bytes 10076160 | tf_op jit(solution)/shard_map/hqk,khd->qhd/dot_general | solution.py:41
  29.6 10.0 %copy.31 = f32[256,1,2048]{0,1,2:T(1,128)} copy(f32[256,1,2048]{0,2,1:T(8,128)S(1)} %bitcast.48) | data formatting | bytes 4194304 | tf_op jit(solution)/shard_map/reshape | solution.py:67
  39.6 5.1 %all-to-all-start = ((f32[256,1,2048]{0,1,2:T(1,128)}), f32[256,1,2048]{0,1,2:T(1,128)}, u32[]{:S(2)}, u32[]{:S(2)}) async-start(f32[256,1,2048]{0,1,2:T(1,128)} %copy.31), calls=%async_computation | async-start | bytes 4194304 | tf_op jit(solution)/shard_map/all_to_all | solution.py:73
  44.9 0.1 copy.34
  45.0 0.3 div.12
  45.4 0.2 div.13
  45.6 46.3 %all-to-all-done = f32[256,1,2048]{0,1,2:T(1,128)} async-done(((f32[256,1,2048]{0,1,2:T(1,128)}), f32[256,1,2048]{0,1,2:T(1,128)}, u32[]{:S(2)}, u32[]{:S(2)}) %all-to-all-start) | async-done | bytes 2097184 | tf_op jit(solution)/shard_map/all_to_all | solution.py:73
  91.9 0.2 mul.38
  92.1 2.0 %fusion.8 = f32[256,512]{0,1:T(8,128)S(1)} fusion(f32[256,1,4,512]{0,3,2,1:T(8,128)S(1)} %bitcast.47, f32[256,1,4,512]{0,1,3,2:T(1,128)} %bitcast.5), kind=kLoop, calls=%fused_computation.10 | loop fusion | flops 917504 | bytes 4718592 | tf_op jit(solution)/shard_map/reduce_sum | solution.py:19
  94.1 0.2 copy.33
  94.3 0.1 fusion.14
  94.4 0.1 copy.35
  94.5 10.5 %all_to_all.51 = bf16[32,8,512]{2,0,1:T(8,128)(2,1)S(1)} all-to-all(bf16[32,8,512]{2,0,1:T(8,128)(2,1)S(1)} %copy.35), channel_id=1, replica_groups=mesh['ctx'=4,'row'=8] {'row'}, dimensions={1} | all-to-all | bytes 524288 | tf_op jit(solution)/shard_map/all_to_all | solution.py:80
  105.0 0.7 copy.57
  (15 shorter events, 0.3 us)
Async XLA Ops:
  0.0 2.0 %copy-start = (bf16[384,2048]{1,0:T(8,128)(2,1)S(1)}, bf16[384,2048]{1,0:T(8,128)(2,1)}, u32[]{:S(2)}) copy-start(bf16[384,2048]{1,0:T(8,128)(2,1)} %param.6) | copy-start | bytes 4718596
  7.9 12.5 %all-to-all-start.1 = ((f32[256,1,16]{0,1,2:T(1,128)}), f32[256,1,16]{0,1,2:T(1,128)S(1)}, u32[]{:S(2)}, u32[]{:S(2)}) async-start(f32[256,1,16]{0,1,2:T(1,128)} %broadcast_in_dim.47), calls=%async_computation.1 | async-start | bytes 32768 | tf_op jit(solution)/shard_map/all_to_all | solution.py:71
  14.2 4.0 %copy-start.1 = (bf16[384,2048]{1,0:T(8,128)(2,1)S(1)}, bf16[384,2048]{1,0:T(8,128)(2,1)}, u32[]{:S(2)}) copy-start(bf16[384,2048]{1,0:T(8,128)(2,1)} %param.7) | copy-start | bytes 4718596
  20.3 19.3 %all-to-all-start.2 = ((f32[256,1,16]{0,1,2:T(1,128)}), f32[256,1,16]{0,1,2:T(1,128)S(1)}, u32[]{:S(2)}, u32[]{:S(2)}) async-start(f32[256,1,16]{0,1,2:T(1,128)} %broadcast_in_dim.48), calls=%async_computation.2 | async-start | bytes 32768 | tf_op jit(solution)/shard_map/all_to_all | solution.py:72
  39.6 52.3 %all-to-all-start = ((f32[256,1,2048]{0,1,2:T(1,128)}), f32[256,1,2048]{0,1,2:T(1,128)}, u32[]{:S(2)}, u32[]{:S(2)}) async-start(f32[256,1,2048]{0,1,2:T(1,128)} %copy.31), calls=%async_computation | async-start | bytes 4194304 | tf_op jit(solution)/shard_map/all_to_all | solution.py:73
where the time goes:
time: 106 us
  waiting for transfers between devices  46.3 us (44%)
  starting transfers between devices  16.5 us (16%)
  local copies, waits for them, and re-layouts  15 us (14%)
  blocking collectives  10.5 us (10%)
  matrix products  9.4 us (9%)
  other arithmetic  7.93 us (7%)
    all_to_all x1, waiting for transfers between devices, local(): lax.all_to_all(sent[2], 'ctx', split_axis=2, concat_axis=1, tiled=True)  46.3 us
    all_to_all x1, blocking collectives, local(): lax.all_to_all(grouped, 'row', split_axis=1, concat_axis=0, tiled=True)  10.5 us
    reshape x1, local copies, waits for them, and re-layouts, local(): seg_out.reshape(row_count, 1, HEADS * HEAD_DIM)  10 us
    all_to_all x1, starting transfers between devices, local(): lax.all_to_all(sent[0], 'ctx', split_axis=2, concat_axis=1, tiled=True)  6.32 us
    dot_general x1, matrix products, segment_parts(): jnp.einsum('qhd,khd->hqk', query_heads, key_heads, preferred_element_type...  5.2 us
    all_to_all x1, starting transfers between devices, local(): lax.all_to_all(sent[2], 'ctx', split_axis=2, concat_axis=1, tiled=True)  5.09 us
    all_to_all x1, starting transfers between devices, local(): lax.all_to_all(sent[1], 'ctx', split_axis=2, concat_axis=1, tiled=True)  5.09 us
    dot_general x1, matrix products, segment_parts(): jnp.einsum('hqk,khd->qhd', probs_low, value_heads, preferred_element_type...  4.2 us
  transfers between devices with their start and end apart: 3, of which 1 were waited for; matrix products, arithmetic and copies ran while one was open for 20% of the time, Pallas kernels for 0%

commit v1 on v0

--- a/solution.py
+++ b/solution.py
@@ -7,6 +7,19 @@
 HEAD_DIM = 128
 BLOCK = 128
 masked_fill = -1e30
+
+
+def _save_object(piece_in, dim_no, own_rows):
+    out_arr, shaped = (piece_in.shape[:dim_no], piece_in.shape[dim_no + 1 :])
+    work_now = jnp.moveaxis(piece_in.reshape(*out_arr, own_rows, -1, *shaped), dim_no, 0)
+    return work_now
+
+
+def _work_tracks(x_part, d0):
+    fresh = list(x_part.shape[1:])
+    fresh[d0] *= x_part.shape[0]
+    n_now = jnp.moveaxis(x_part, 0, d0).reshape(fresh)
+    return n_now
 
 
 def combine_rows(pieces):
@@ -66,11 +79,29 @@
         jnp.transpose(seg_total)[:, None, :],
         seg_out.reshape(row_count, 1, HEADS * HEAD_DIM),
     )
+
+    def compute_the_sums_all(mine_x, lane_axis, arr_in, local_values):
+        prior, then = (jax.lax.psum(1, axis_name=lane_axis), jax.lax.axis_index(lane_axis))
+        carry_out = _save_object(mine_x, arr_in, prior)
+        entries = [carry_out[then]]
+        ix = 1
+        while ix < prior:
+            base_arr = carry_out[then ^ ix]
+            entries.append(
+                jax.lax.ppermute(
+                    base_arr, axis_name=lane_axis, perm=[(k0, k0 ^ ix) for k0 in range(prior)]
+                )
+            )
+            ix += 1
+        carry_out = jnp.stack(entries)[then ^ jnp.arange(prior)]
+        step_out = _work_tracks(carry_out, local_values)
+        return step_out
+
     attended = combine_rows(
         (
             lax.all_to_all(sent[0], "ctx", split_axis=2, concat_axis=1, tiled=True),
             lax.all_to_all(sent[1], "ctx", split_axis=2, concat_axis=1, tiled=True),
-            lax.all_to_all(sent[2], "ctx", split_axis=2, concat_axis=1, tiled=True),
+            compute_the_sums_all(sent[2], "ctx", 2, 1),
         )
     )
     attended_low = attended.astype(jnp.bfloat16)

time: 106 us -> 91.4 us (0.86)
  waiting for transfers between devices: 46.3 us -> 36.6 us
  local copies, waits for them, and re-layouts: 15 us -> 9.6 us
    all_to_all x1 -> x0, waiting for transfers between devices: 46.3 us -> none  [local(): lax.all_to_all(sent[2], 'ctx', split_axis=2, concat_axis=1, tiled=True)]
    all_to_all x1, waiting for transfers between devices: 0.01 us -> 36.6 us  [local(): lax.all_to_all(sent[1], 'ctx', split_axis=2, concat_axis=1, tiled=True)]
    reshape x1 -> x0, local copies, waits for them, and re-layouts: 10 us -> none  [local(): seg_out.reshape(row_count, 1, HEADS * HEAD_DIM)]
    all_to_all x1 -> x0, starting transfers between devices: 5.09 us -> none  [local(): lax.all_to_all(sent[2], 'ctx', split_axis=2, concat_axis=1, tiled=True)]
    ppermute x0 -> x3, starting transfers between devices: none -> 4.39 us  [compute_the_sums_all(): jax.lax.ppermute(base_arr, axis_name=lane_axis, perm=[(k0, k0 ^ ix) for k...]
    gather x0 -> x1, local copies, waits for them, and re-layouts: none -> 3.56 us  [compute_the_sums_all(): carry_out = jnp.stack(entries)[then ^ jnp.arange(prior)]]
    another operation x0 -> x1, other arithmetic: none -> 2.88 us  [compute_the_sums_all(): carry_out = jnp.stack(entries)[then ^ jnp.arange(prior)]]
    reduce_sum x1, other arithmetic: 3.96 us -> 2.02 us  [segment_parts(): seg_total = jnp.sum(probs_live, axis=2)]
  transfers between devices with their start and end apart: 3 -> 5, of which waited for: 1 -> 1; matrix products, arithmetic and copies ran while one was open for 20% -> 12% of each run, Pallas kernels for 0% -> 0%
where the time goes in v1:
time: 91.4 us; the launch traced here: 90.9 us
  waiting for transfers between devices  36.6 us (40%)
  starting transfers between devices  15.8 us (17%)
  blocking collectives  10.5 us (11%)
  matrix products  9.65 us (11%)
  local copies, waits for them, and re-layouts  9.6 us (11%)
  other arithmetic  8.64 us (9%)
    all_to_all x1, waiting for transfers between devices, local(): lax.all_to_all(sent[1], 'ctx', split_axis=2, concat_axis=1, tiled=True)  36.6 us
    all_to_all x1, blocking collectives, local(): lax.all_to_all(grouped, 'row', split_axis=1, concat_axis=0, tiled=True)  10.5 us
    all_to_all x1, starting transfers between devices, local(): lax.all_to_all(sent[0], 'ctx', split_axis=2, concat_axis=1, tiled=True)  6.32 us
    dot_general x1, matrix products, segment_parts(): jnp.einsum('qhd,khd->hqk', query_heads, key_heads, preferred_element_type...  5.32 us
    all_to_all x1, starting transfers between devices, local(): lax.all_to_all(sent[1], 'ctx', split_axis=2, concat_axis=1, tiled=True)  5.09 us
    ppermute x3, starting transfers between devices, compute_the_sums_all(): jax.lax.ppermute(base_arr, axis_name=lane_axis, perm=[(k0, k0 ^ ix) for k...  4.39 us
    dot_general x1, matrix products, segment_parts(): jnp.einsum('hqk,khd->qhd', probs_low, value_heads, preferred_element_type...  4.33 us
    gather x1, local copies, waits for them, and re-layouts, compute_the_sums_all(): carry_out = jnp.stack(entries)[then ^ jnp.arange(prior)]  3.56 us
  transfers between devices with their start and end apart: 5, of which 1 were waited for; matrix products, arithmetic and copies ran while one was open for 12% of the time, Pallas kernels for 0%

profile of v1, /device:TPU:0, one launch (start us, length us, event | category | flops | bytes accessed | tf_op | source)
XLA Modules:
  0.0 90.9 jit_solution(3181847861668207893)
XLA Ops:
  0.0 0.8 iota_compare_fusion
  0.9 0.9 and_reduce_fusion
  1.8 0.2 copy.25
  2.1 5.3 %select_reduce_fusion = (f32[16,256]{1,0:T(8,128)S(1)}, f32[16,256,384]{2,1,0:T(8,128)}) fusion(pred[256,384]{1,0:T(8,128)(4,1)S(1)} %copy.25, bf16[384,2048]{1,0:T(8,128)(2,1)S(1)} %copy-done, bf16[256,2048]{1,0:T(8,128)(2,1)} %param.5), kind=kOutput, calls=%fused_computation.2 | convolution fusion | flops 407367680 | bytes 9027584 | tf_op jit(solution)/shard_map/qhd,khd->hqk/dot_general | solution.py:47
  7.4 0.6 broadcast_in_dim.48
  8.0 6.3 %all-to-all-start = ((f32[256,1,16]{0,1,2:T(1,128)}), f32[256,1,16]{0,1,2:T(1,128)S(1)}, u32[]{:S(2)}, u32[]{:S(2)}) async-start(f32[256,1,16]{0,1,2:T(1,128)} %broadcast_in_dim.48), calls=%async_computation | async-start | bytes 32768 | tf_op jit(solution)/shard_map/all_to_all | solution.py:102
  14.3 1.6 %copy.32 = bf16[384,2048]{0,1:T(8,128)(2,1)} copy(bf16[384,2048]{1,0:T(8,128)(2,1)S(1)} %copy-done.1) | data formatting | bytes 3145728 | tf_op jit(solution)/shard_map/reshape | solution.py:66
  15.9 4.3 %fusion.2 = f32[16,256,128]{1,2,0:T(8,128)S(1)} fusion(bf16[384,16,128]{0,2,1:T(8,128)(2,1)} %bitcast.71, f32[16,256,384]{2,1,0:T(8,128)} %get-tuple-element.12, f32[16,256]{1,0:T(8,128)S(1)} %get-tuple-element.11, pred[256,384]{1,0:T(8,128)(4,1)S(1)} %copy.25), kind=kOutput, calls=%fused_computation.5 | convolution fusion | flops 408944640 | bytes 10076160 | tf_op jit(solution)/shard_map/hqk,khd->qhd/dot_general | solution.py:54
  20.2 1.2 %dynamic-slice_bitcast_fusion.3 = (f32[1,256,1,512]{1,3,2,0:T(8,128)S(1)}, f32[256,1,512]{0,2,1:T(8,128)}, f32[256,1,512]{0,2,1:T(8,128)}, f32[256,1,512]{0,2,1:T(8,128)}) fusion(f32[256,1,4,512]{0,3,2,1:T(8,128)S(1)} %bitcast.70, s32[]{:T(128)S(6)} %select_n.31, s32[]{:T(128)S(6)} %select_n.34, s32[]{:T(128)S(6)} %select_n.33, s32[]{:T(128)S(6)} %select_n.32), kind=kLoop, calls=%fused_computation.23 | loop fusion | bytes 4194320 | tf_op jit(solution)/shard_map/dynamic_slice | solution.py:86
  21.4 3.8 %collective-permute-start.2 = (f32[256,1,512]{0,2,1:T(8,128)}, f32[256,1,512]{0,2,1:T(8,128)}, u32[]{:S(2)}, u32[]{:S(2)}) collective-permute-start(f32[256,1,512]{0,2,1:T(8,128)} %get-tuple-element.8), channel_id=1, source_target_pairs={{0,24},{8,16},{16,8},{24,0},{1,25},{9,17},{17,9},{25,1},{2,26},{10... | collective-permute-start | bytes 1572872 | tf_op jit(solution)/shard_map/ppermute | solution.py:91
  25.3 0.6 collective-permute-start
  25.8 2.0 %fusion = f32[16,256]{1,0:T(8,128)S(1)} fusion(f32[16,256,384]{2,1,0:T(8,128)S(1)} %bitcast.69, f32[16,256]{1,0:T(8,128)S(1)} %get-tuple-element.11, pred[256,384]{1,0:T(8,128)(4,1)S(1)} %copy.25), kind=kLoop, calls=%fused_computation.3 | loop fusion | flops 6287360 | bytes 6422528 | tf_op jit(solution)/shard_map/reduce_sum | solution.py:52
  27.9 0.6 broadcast_in_dim.49
  28.5 5.1 %all-to-all-start.1 = ((f32[256,1,16]{0,1,2:T(1,128)}), f32[256,1,16]{0,1,2:T(1,128)S(1)}, u32[]{:S(2)}, u32[]{:S(2)}) async-start(f32[256,1,16]{0,1,2:T(1,128)} %broadcast_in_dim.49), calls=%async_computation.1 | async-start | bytes 32768 | tf_op jit(solution)/shard_map/all_to_all | solution.py:103
  33.7 36.6 %all-to-all-done.1 = f32[256,1,16]{0,1,2:T(1,128)S(1)} async-done(((f32[256,1,16]{0,1,2:T(1,128)}), f32[256,1,16]{0,1,2:T(1,128)S(1)}, u32[]{:S(2)}, u32[]{:S(2)}) %all-to-all-start.1) | async-done | bytes 16416 | tf_op jit(solution)/shard_map/all_to_all | solution.py:103
  70.4 0.1 copy.30
  70.5 0.3 div.12
  70.9 0.2 div.13
  71.1 2.9 %maximum_bitcast_fusion = f32[4,256,512]{1,2,0:T(8,128)} fusion(f32[1,256,1,512]{1,3,2,0:T(8,128)} %bitcast.12, f32[1,256,1,512]{1,3,2,0:T(8,128)} %bitcast.10, f32[1,256,1,512]{1,3,2,0:T(8,128)} %bitcast.8, f32[1,256,1,512]{1,3,2,0:T(8,128)S(1)} %get-tuple-element.7), kind=kLoop, calls=%fused_computation.10 | loop fusion | flops 1572864 | bytes 4194304 | tf_op jit(solution)/shard_map/stack | solution.py:96
  74.0 3.6 %gather_fusion = f32[4,256,512]{1,2,0:T(8,128)} fusion(f32[4,256,512]{1,2,0:T(8,128)} %maximum_bitcast_fusion, s32[1024]{0:T(1024)S(1)} %pad_clamp_fusion), kind=kCustom, calls=%fused_computation | custom fusion | bytes 4194320 | tf_op jit(solution)/shard_map/gather | solution.py:96
  77.6 1.8 %fusion.8 = f32[256,512]{0,1:T(8,128)S(1)} fusion(f32[4,256,512]{1,2,0:T(8,128)} %gather_fusion, f32[256,4,4]{0,2,1:T(4,128)S(1)} %get-tuple-element.6), kind=kLoop, calls=%fused_computation.12 | loop fusion | flops 917504 | bytes 2637824 | tf_op jit(solution)/shard_map/reduce_sum | solution.py:32
  79.4 0.2 copy.29
  79.8 10.5 %all_to_all.39 = bf16[32,8,512]{2,0,1:T(8,128)(2,1)S(1)} all-to-all(bf16[32,8,512]{2,0,1:T(8,128)(2,1)S(1)} %copy.31), channel_id=1, replica_groups=mesh['ctx'=4,'row'=8] {'row'}, dimensions={1} | all-to-all | bytes 524288 | tf_op jit(solution)/shard_map/all_to_all | solution.py:111
  90.2 0.7 copy.50
  (27 shorter events, 0.5 us)
Async XLA Ops:
  0.0 2.0 %copy-start = (bf16[384,2048]{1,0:T(8,128)(2,1)S(1)}, bf16[384,2048]{1,0:T(8,128)(2,1)}, u32[]{:S(2)}) copy-start(bf16[384,2048]{1,0:T(8,128)(2,1)} %param.6) | copy-start | bytes 4718596
  2.0 12.3 %copy-start.1 = (bf16[384,2048]{1,0:T(8,128)(2,1)S(1)}, bf16[384,2048]{1,0:T(8,128)(2,1)}, u32[]{:S(2)}) copy-start(bf16[384,2048]{1,0:T(8,128)(2,1)} %param.7) | copy-start | bytes 4718596
  8.0 20.5 %all-to-all-start = ((f32[256,1,16]{0,1,2:T(1,128)}), f32[256,1,16]{0,1,2:T(1,128)S(1)}, u32[]{:S(2)}, u32[]{:S(2)}) async-start(f32[256,1,16]{0,1,2:T(1,128)} %broadcast_in_dim.48), calls=%async_computation | async-start | bytes 32768 | tf_op jit(solution)/shard_map/all_to_all | solution.py:102
  15.9 10.0 %slice-start = ((s8[6291456]{0:T(1024)(128)(4,1)}), s8[4194304]{0:T(1024)(128)(4,1)S(1)}, s32[]{:S(2)}) async-start(s8[6291456]{0:T(1024)(128)(4,1)} %bitcast.68), calls=%async_computation.3 | async-start | bytes 8388608
  15.9 10.0 %slice-start.1 = ((s8[6291456]{0:T(1024)(128)(4,1)}), s8[2097152]{0:T(1024)(128)(4,1)S(1)}, s32[]{:S(2)}) async-start(s8[6291456]{0:T(1024)(128)(4,1)} %bitcast.68), calls=%async_computation.4 | async-start | bytes 4194304
  21.4 49.7 %collective-permute-start.2 = (f32[256,1,512]{0,2,1:T(8,128)}, f32[256,1,512]{0,2,1:T(8,128)}, u32[]{:S(2)}, u32[]{:S(2)}) collective-permute-start(f32[256,1,512]{0,2,1:T(8,128)} %get-tuple-element.8), channel_id=1, source_target_pairs={{0,24},{8,16},{16,8},{24,0},{1,25},{9,17},{17,9},{25,1},{2,26},{10... | collective-permute-start | bytes 1572872 | tf_op jit(solution)/shard_map/ppermute | solution.py:91
  25.3 45.8 %collective-permute-start.1 = (f32[256,1,512]{0,2,1:T(8,128)}, f32[256,1,512]{0,2,1:T(8,128)}, u32[]{:S(2)}, u32[]{:S(2)}) collective-permute-start(f32[256,1,512]{0,2,1:T(8,128)} %get-tuple-element.9), channel_id=1, source_target_pairs={{0,16},{8,24},{16,0},{24,8},{1,17},{9,25},{17,1},{25,9},{2,18},{10... | collective-permute-start | bytes 1572872 | tf_op jit(solution)/shard_map/ppermute | solution.py:91
  25.3 45.9 %collective-permute-start = (f32[256,1,512]{0,2,1:T(8,128)}, f32[256,1,512]{0,2,1:T(8,128)}, u32[]{:S(2)}, u32[]{:S(2)}) collective-permute-start(f32[256,1,512]{0,2,1:T(8,128)} %get-tuple-element.10), channel_id=1, source_target_pairs={{0,8},{8,0},{16,24},{24,16},{1,9},{9,1},{17,25},{25,17},{2,10},{10... | collective-permute-start | bytes 1572872 | tf_op jit(solution)/shard_map/ppermute | solution.py:91
  28.5 41.8 %all-to-all-start.1 = ((f32[256,1,16]{0,1,2:T(1,128)}), f32[256,1,16]{0,1,2:T(1,128)S(1)}, u32[]{:S(2)}, u32[]{:S(2)}) async-start(f32[256,1,16]{0,1,2:T(1,128)} %broadcast_in_dim.49), calls=%async_computation.1 | async-start | bytes 32768 | tf_op jit(solution)/shard_map/all_to_all | solution.py:103
